TPU v7x, 32 devices: a whole 2x2x4 slice. The times are simulated.
32 devices in a mesh: grp: 4 (over x, core), rel: 8 (over z, y).
Axes of the slice: x: 2, y: 2, z: 4, core: 2. Of those that a mesh axis runs over, the one named last changes fastest.
Arguments:
- head_ids: int32 [65536], P(('grp', 'rel')), may hold values from 0 to 1023
- relations: int32 [65536, 1], P(('grp', 'rel')), may hold values from 0 to 31; in each aligned block of 2048 rows (0 to 2047, 2048 to 4095, ...) at most 128 rows name the same one
- tail_ids: int32 [65536], P(('grp', 'rel')), may hold values from 0 to 1023
- neg_owner: int32 [1], replicated, may hold values from 0 to 31
- entities: bfloat16 [32768, 512], P(('grp', 'rel')), may hold values from -0.3984375 to 0.3984375
- rel_weight: float32 [32, 512, 512], P('rel'), may hold values from -6 to 6
- rel_accum: float32 [32, 512], P('rel'), may hold values from 0.001 to 0.1
Outputs:
- losses: bfloat16 [65536], P(('grp', 'rel'))
- head_grad: bfloat16 [65536, 512], P(('grp', 'rel'))
- new_rel: float32 [32, 512, 512], P('rel')
- new_accum: float32 [32, 512], P('rel')
Inputs may be any that keep to these rules, and one draw needn't show every extreme that they name: `head_ids`: a row of the device's own shard of 1024 entity rows. `tail_ids`: a row of the device's own shard of 1024 entity rows. `relations`: in the 2048 rows of one device no relation is named by more than 128 rows; some relation is named by exactly 128. `neg_owner`: a device index, counted grp first, then rel.
All inputs are finite; a program needn't handle non-finite values.
Results may differ from a plain program's by a relative error of at most 0.0095.
Values may be sent and summed in bfloat16 or wider, within the bound.
No kernel may reach another device: no remote copies, remote signals or barrier semaphores. Data moves between devices by JAX's collectives and lax.ppermute only.
A program may use at most 128 MiB of HBM per device.

v0:
```python
import jax
import jax.numpy as jnp
from jax import lax
from jax.sharding import PartitionSpec as P

LEARNING_RATE = 1.0


def broadcast(shard, axis, root):
    mine = lax.axis_index(axis) == root
    return lax.psum(jnp.where(mine, shard, jnp.zeros_like(shard)), axis)


def slot_ranks(rel_ids, bucket_count):
    one_hot = (rel_ids[..., None] == jnp.arange(bucket_count, dtype=jnp.int32)).astype(jnp.int32)
    running = jnp.cumsum(one_hot, axis=-2) - 1
    return jnp.sum(one_hot * running, axis=-1)


def score_rows(query_rows, tail_rows, negatives):
    positive = jnp.sum(query_rows.astype(jnp.float32) * tail_rows.astype(jnp.float32), axis=-1)
    neg_scores = jnp.dot(query_rows, negatives.T, preferred_element_type=jnp.float32)
    losses = jax.nn.softplus(-positive) + jnp.mean(jax.nn.softplus(neg_scores), axis=-1)
    coefs = (jax.nn.sigmoid(neg_scores) / negatives.shape[0]).astype(jnp.bfloat16)
    grad_query = -jax.nn.sigmoid(-positive)[:, None] * tail_rows.astype(jnp.float32)
    grad_query = grad_query + jnp.dot(coefs, negatives, preferred_element_type=jnp.float32)
    return (losses.astype(jnp.bfloat16), grad_query.astype(jnp.bfloat16))


def adagrad(weight, accumulator, gradient):
    new_accum = accumulator + jnp.mean(gradient * gradient, axis=-1)
    return (weight - LEARNING_RATE * gradient / jnp.sqrt(new_accum)[..., None], new_accum)


def to_buckets(values, position, layout):
    flat_shape = (layout[0] * layout[1] * layout[2],) + values.shape[1:]
    filled = jnp.zeros(flat_shape, values.dtype).at[position].set(values)
    return filled.reshape(layout + values.shape[1:])


def from_buckets(stacked, position):
    return stacked.reshape((-1,) + stacked.shape[3:])[position]


def per_device(head_ids, relations, tail_ids, neg_owner, entities, rel_weight, rel_accum):
    rows_here = head_ids.shape[0]
    width = entities.shape[1]
    owner_count = lax.axis_size("rel")
    local_rels = rel_weight.shape[0]
    capacity = 2 * rows_here // (owner_count * local_rels)
    layout = (owner_count, local_rels, capacity)
    rel_ids = relations[:, 0]
    position = rel_ids * capacity + slot_ranks(rel_ids, owner_count * local_rels)
    head_rows = jnp.take(entities, head_ids, axis=0)
    tail_rows = jnp.take(entities, tail_ids, axis=0)
    matrices = rel_weight.astype(jnp.bfloat16)
    negatives = broadcast(entities, ("grp", "rel"), neg_owner[0])
    held_rows, held_tails = (
        lax.all_to_all(
            to_buckets(head_rows, position, layout), "rel", split_axis=0, concat_axis=0, tiled=True
        ),
        lax.all_to_all(
            to_buckets(tail_rows, position, layout), "rel", split_axis=0, concat_axis=0, tiled=True
        ),
    )
    projected = jnp.einsum(
        "srcd,rde->srce", held_rows, matrices, preferred_element_type=jnp.float32
    ).astype(jnp.bfloat16)
    slot_losses, slot_grads = score_rows(
        projected.reshape(-1, width), held_tails.reshape(-1, width), negatives
    )
    grad_rows = slot_grads.reshape(held_rows.shape)
    partial_value = jnp.einsum(
        "srcd,srce->rde", held_rows, grad_rows, preferred_element_type=jnp.float32
    )
    head_back = jnp.einsum(
        "srce,rde->srcd", grad_rows, matrices, preferred_element_type=jnp.float32
    ).astype(jnp.bfloat16)
    partial_value, head_back = (partial_value, head_back)
    back_grads, back_losses = (
        lax.all_to_all(head_back, "rel", split_axis=0, concat_axis=0, tiled=True),
        lax.all_to_all(slot_losses.reshape(layout), "rel", split_axis=0, concat_axis=0, tiled=True),
    )
    head_grad = from_buckets(back_grads, position)
    losses = from_buckets(back_losses, position)
    summed = lax.psum(partial_value.astype(jnp.bfloat16), "grp").astype(jnp.float32)
    new_rel, new_accum = adagrad(rel_weight, rel_accum, summed)
    return (losses, head_grad, new_rel, new_accum)


def solution(mesh):
    placed = (
        P(("grp", "rel")),
        P(("grp", "rel"), None),
        P(("grp", "rel")),
        P(),
        P(("grp", "rel"), None),
        P("rel", None, None),
        P("rel", None),
    )
    return jax.shard_map(
        per_device,
        mesh=mesh,
        in_specs=placed,
        out_specs=(
            P(("grp", "rel")),
            P(("grp", "rel"), None),
            P("rel", None, None),
            P("rel", None),
        ),
        check_vma=False,
    )
```

profile of v0, /device:TPU:0, one launch (start us, length us, event | category | flops | bytes accessed | tf_op | source)
XLA Modules:
  0.0 504.7 jit_solution(10861121189316165478)
XLA Ops:
  7.2 0.7 compare_and_fusion
  7.9 0.7 fusion.34
  8.6 0.7 fusion.30
  9.3 9.1 %reduce-window.6 = s32[32,16,128]{2,1,0:T(8,128)S(1)} reduce-window(s32[32,16,128]{2,1,0:T(8,128)S(1)} %fusion.30, s32[]{:T(128)} %constant.22.clone.1), window={size=1x1x128 pad=0_0x0_0x127_0}, to_apply=%region_0.0 | reduce-window | flops 8323072 | bytes 524292 | tf_op jit(solution)/shard_map/reduce-window
  19.1 0.8 fusion.29
  19.9 0.7 compare_select_fusion.1
  20.6 27.7 %scatter_custom_fusion.1 = bf16[4096,512]{1,0:T(8,128)(2,1)} fusion(s32[2048]{0:T(1024)S(1)} %bitcast.69, bf16[]{:T(256)} %constant.20.clone.1, pred[2048]{0:T(1024)(128)(4,1)S(1)} %compare_and_fusion, bf16[]{:T(256)} %constant.15.clone.2, bf16[1024,512]{1,0:T(8,128)(2,1)} %param.13, s32[2048]{0:T(1024)S(1)} %fusion.34), kind=kCustom, calls=%fused_computation.28 | custom fusion | flops 1048576 | bytes 5253124 | tf_op jit(solution)/shard_map/scatter | solution.py:37
  48.3 7.4 %all-to-all-start.1 = ((bf16[8,4,128,512]{3,2,1,0:T(8,128)(2,1)}), bf16[8,4,128,512]{3,2,1,0:T(8,128)(2,1)}, u32[]{:S(2)}, u32[]{:S(2)}) async-start(bf16[8,4,128,512]{3,2,1,0:T(8,128)(2,1)} %bitcast.60), calls=%async_computation.1 | async-start | bytes 8388608 | tf_op jit(solution)/shard_map/all_to_all | solution.py:62
  55.8 22.6 %scatter_custom_fusion = bf16[4096,512]{1,0:T(8,128)(2,1)} fusion(s32[2048]{0:T(1024)S(1)} %bitcast.70, bf16[]{:T(256)} %constant.20.clone.1, pred[2048]{0:T(1024)(128)(4,1)S(1)} %compare_and_fusion.1, bf16[]{:T(256)} %constant.15.clone.2, bf16[1024,512]{1,0:T(8,128)(2,1)S(1)} %copy-done, s32[2048]{0:T(1024)S(1)} %fusion.33), kind=kCustom, calls=%fused_computation.30 | custom fusion | flops 1048576 | bytes 5253124 | tf_op jit(solution)/shard_map/scatter | solution.py:37
  78.4 70.6 %all-to-all-done.1 = bf16[8,4,128,512]{3,2,1,0:T(8,128)(2,1)} async-done(((bf16[8,4,128,512]{3,2,1,0:T(8,128)(2,1)}), bf16[8,4,128,512]{3,2,1,0:T(8,128)(2,1)}, u32[]{:S(2)}, u32[]{:S(2)}) %all-to-all-start.1) | async-done | bytes 4194336 | tf_op jit(solution)/shard_map/all_to_all | solution.py:62
  149.0 4.6 all-to-all-start
  154.6 1.0 broadcast_select_fusion
  155.6 95.5 %all-to-all-done = bf16[8,4,128,512]{3,2,1,0:T(8,128)(2,1)} async-done(((bf16[8,4,128,512]{3,2,1,0:T(8,128)(2,1)}), bf16[8,4,128,512]{3,2,1,0:T(8,128)(2,1)}, u32[]{:S(2)}, u32[]{:S(2)}) %all-to-all-start) | async-done | bytes 4194336 | tf_op jit(solution)/shard_map/all_to_all | solution.py:59
  251.2 7.2 %multiply_reduce_fusion = (f32[8,4,128]{2,0,1:T(8,128)S(1)}, bf16[8,4,128,512]{3,2,0,1:T(8,128)(2,1)S(1)}) fusion(bf16[8,4,128,512]{3,2,1,0:T(8,128)(2,1)} %all-to-all-done.1, f32[4,512,512]{2,1,0:T(8,128)} %param.14, bf16[8,4,128,512]{3,2,1,0:T(8,128)(2,1)} %all-to-all-done), kind=kOutput, calls=%fused_computation.12 | convolution fusion | flops 2159013888 | bytes 16793600 | tf_op jit(solution)/shard_map/srcd,rde->srce/dot_general | solution.py:66
  258.3 2.5 copy.50
  260.8 3.4 copy_convert_fusion
  264.2 4.2 copy.54
  268.4 82.8 %all-reduce.3.cloned.1.call-done = bf16[1024,512]{1,0:T(8,128)(2,1)} async-done(((bf16[1024,512]{1,0:T(8,128)(2,1)}), bf16[1024,512]{1,0:T(8,128)(2,1)}) %all-reduce.3.cloned.1.call-update) | async-done | bytes 1048592 | tf_op jit(solution)/shard_map/psum | solution.py:11
  351.3 16.5 %fusion = (f32[4096]{0:T(1024)S(1)}, f32[4096,1024]{0,1:T(8,128)}) fusion(bf16[4096,512]{1,0:T(8,128)(2,1)} %bitcast.61, bf16[1024,512]{1,0:T(8,128)(2,1)} %all-reduce.3.cloned.1.call-done), kind=kOutput, calls=%fused_computation.7 | convolution fusion | flops 4324323328 | bytes 22036480 | tf_op jit(solution)/shard_map/dot_general | solution.py:22
  368.4 4.4 all-to-all-start.2
  372.8 11.3 %fusion.2 = bf16[4096,512]{1,0:T(8,128)(2,1)S(1)} fusion(f32[8,4,128,512]{3,2,1,0:T(8,128)} %copy.54, bf16[1024,512]{1,0:T(8,128)(2,1)S(1)} %copy-done.4, f32[4096,1024]{0,1:T(8,128)} %get-tuple-element.12, f32[4096]{0:T(1024)S(1)} %bitcast.72), kind=kOutput, calls=%fused_computation.11 | convolution fusion | flops 4322230272 | bytes 30425088 | tf_op jit(solution)/shard_map/dot_general | solution.py:26
  384.2 2.4 convert_bitcast_fusion
  386.6 2.2 copy.56
  388.8 6.0 %all-to-all-start.3 = ((bf16[8,4,128,512]{3,2,1,0:T(8,128)(2,1)}), bf16[8,4,128,512]{3,2,1,0:T(8,128)(2,1)}, u32[]{:S(2)}, u32[]{:S(2)}) async-start(bf16[8,4,128,512]{3,2,1,0:T(8,128)(2,1)} %copy.56), calls=%async_computation.3 | async-start | bytes 8388608 | tf_op jit(solution)/shard_map/all_to_all | solution.py:81
  394.9 7.2 %bitcast_convert_fusion = bf16[4,512,512]{2,1,0:T(8,128)(2,1)} fusion(bf16[8,4,128,512]{3,2,1,0:T(8,128)(2,1)} %all-to-all-done, bf16[8,4,128,512]{3,2,1,0:T(8,128)(2,1)} %bitcast.74), kind=kOutput, calls=%fused_computation.18 | convolution fusion | flops 2148532224 | bytes 10485760 | tf_op jit(solution)/shard_map/srcd,srce->rde/dot_general | solution.py:73
  402.1 22.1 %gather_fusion = bf16[2048]{0:T(1024)(128)(2,1)} fusion(bf16[4096]{0:T(1024)(128)(2,1)S(1)} %bitcast.58, s32[2048]{0:T(1024)S(1)} %broadcast_clamp_fusion), kind=kCustom, calls=%fused_computation.2 | custom fusion | bytes 16384 | tf_op jit(solution)/shard_map/gather | solution.py:42
  424.2 29.9 %all-reduce.5.cloned.1.call-done = bf16[4,512,512]{2,1,0:T(8,128)(2,1)} async-done(((bf16[4,512,512]{2,1,0:T(8,128)(2,1)}), bf16[4,512,512]{2,1,0:T(8,128)(2,1)}) %all-reduce.5.cloned.1.call-update) | async-done | bytes 2097168 | tf_op jit(solution)/shard_map/psum | solution.py:86
  454.1 2.1 fusion.4
  456.2 0.6 fusion.39
  456.8 5.5 %fusion.5 = f32[4,512,512]{2,1,0:T(8,128)} fusion(f32[4,512,512]{2,1,0:T(8,128)} %param.14, bf16[4,512,512]{2,1,0:T(8,128)(2,1)} %all-reduce.5.cloned.1.call-done, f32[4,512]{1,0:T(4,128)S(1)} %get-tuple-element.5), kind=kLoop, calls=%fused_computation.17 | loop fusion | flops 3145728 | bytes 10493952 | tf_op jit(solution)/shard_map/sub | solution.py:32
  462.3 23.6 %all-to-all-done.3 = bf16[8,4,128,512]{3,2,1,0:T(8,128)(2,1)} async-done(((bf16[8,4,128,512]{3,2,1,0:T(8,128)(2,1)}), bf16[8,4,128,512]{3,2,1,0:T(8,128)(2,1)}, u32[]{:S(2)}, u32[]{:S(2)}) %all-to-all-start.3) | async-done | bytes 4194336 | tf_op jit(solution)/shard_map/all_to_all | solution.py:81
  485.9 12.0 %gather_fusion.1 = bf16[2048,512]{1,0:T(8,128)(2,1)} fusion(bf16[4096,512]{1,0:T(8,128)(2,1)} %bitcast.21, s32[2048]{0:T(1024)S(1)} %broadcast_clamp_fusion), kind=kCustom, calls=%fused_computation.3 | custom fusion | bytes 4202496 | tf_op jit(solution)/shard_map/gather | solution.py:42
  (28 shorter events, 1.7 us)
Async XLA Ops:
  48.3 7.4 %copy-start.2 = (s32[2048]{0:T(1024)S(1)}, s32[2048]{0:T(1024)}, u32[]{:S(2)}) copy-start(s32[2048]{0:T(1024)} %param.9) | copy-start | bytes 24580
  48.3 7.5 %copy-start = (bf16[1024,512]{1,0:T(8,128)(2,1)S(1)}, bf16[1024,512]{1,0:T(8,128)(2,1)}, u32[]{:S(2)}) copy-start(bf16[1024,512]{1,0:T(8,128)(2,1)} %param.13) | copy-start | bytes 3145732
  48.3 100.7 %all-to-all-start.1 = ((bf16[8,4,128,512]{3,2,1,0:T(8,128)(2,1)}), bf16[8,4,128,512]{3,2,1,0:T(8,128)(2,1)}, u32[]{:S(2)}, u32[]{:S(2)}) async-start(bf16[8,4,128,512]{3,2,1,0:T(8,128)(2,1)} %bitcast.60), calls=%async_computation.1 | async-start | bytes 8388608 | tf_op jit(solution)/shard_map/all_to_all | solution.py:62
  149.0 102.1 %all-to-all-start = ((bf16[8,4,128,512]{3,2,1,0:T(8,128)(2,1)}), bf16[8,4,128,512]{3,2,1,0:T(8,128)(2,1)}, u32[]{:S(2)}, u32[]{:S(2)}) async-start(bf16[8,4,128,512]{3,2,1,0:T(8,128)(2,1)} %bitcast.59), calls=%async_computation | async-start | bytes 8388608 | tf_op jit(solution)/shard_map/all_to_all | solution.py:59
  153.6 197.6 %all-reduce.3.cloned.1.call-start = ((), (), s32[]{:S(2)}) async-start(), calls=%async_computation.4 | async-start | bytes 2097152 | tf_op jit(solution)/shard_map/psum | solution.py:11
  351.2 21.6 %copy-start.4 = (bf16[1024,512]{1,0:T(8,128)(2,1)S(1)}, bf16[1024,512]{1,0:T(8,128)(2,1)}, u32[]{:S(2)}) copy-start(bf16[1024,512]{1,0:T(8,128)(2,1)} %all-reduce.3.cloned.1.call-done) | copy-start | bytes 3145732
  368.4 20.4 %all-to-all-start.2 = ((bf16[8,4,128]{2,1,0:T(4,128)(2,1)}), bf16[8,4,128]{2,1,0:T(4,128)(2,1)S(1)}, u32[]{:S(2)}, u32[]{:S(2)}) async-start(bf16[8,4,128]{2,1,0:T(4,128)(2,1)} %copy.52), calls=%async_computation.2 | async-start | bytes 16384 | tf_op jit(solution)/shard_map/all_to_all | solution.py:82
  372.8 11.3 %copy-start.1 = (f32[4,512,512]{2,1,0:T(8,128)S(1)}, f32[4,512,512]{2,1,0:T(8,128)}, u32[]{:S(2)}) copy-start(f32[4,512,512]{2,1,0:T(8,128)} %param.14) | copy-start | bytes 12582916
  384.2 2.4 copy-start.5
  388.8 97.0 %all-to-all-start.3 = ((bf16[8,4,128,512]{3,2,1,0:T(8,128)(2,1)}), bf16[8,4,128,512]{3,2,1,0:T(8,128)(2,1)}, u32[]{:S(2)}, u32[]{:S(2)}) async-start(bf16[8,4,128,512]{3,2,1,0:T(8,128)(2,1)} %copy.56), calls=%async_computation.3 | async-start | bytes 8388608 | tf_op jit(solution)/shard_map/all_to_all | solution.py:81
  394.8 59.3 %all-reduce.5.cloned.1.call-start = ((), (), s32[]{:S(2)}) async-start(), calls=%async_computation.5 | async-start | bytes 4194304 | tf_op jit(solution)/shard_map/psum | solution.py:86
  402.0 54.1 %copy-start.3 = (f32[4,512]{1,0:T(4,128)S(1)}, f32[4,512]{1,0:T(4,128)}, u32[]{:S(2)}) copy-start(f32[4,512]{1,0:T(4,128)} %param.15) | copy-start | bytes 24580
Sparse Core Ops, SparseCore 0:
  160.2 190.9 all-reduce.2
  402.2 51.8 all-reduce.4
where the time goes:
time: 506 us; the launch traced here: 505 us
  waiting for transfers between devices  303 us (60%)
  other arithmetic  76 us (15%)
  matrix products  44.5 us (9%)
  local copies, waits for them, and re-layouts  44 us (9%)
  starting transfers between devices  22.8 us (5%)
  between operations  14.8 us (3%)
    all_to_all x1, waiting for transfers between devices, per_device(): lax.all_to_all(to_buckets(head_rows, position, layout), 'rel', split_axis...  95.5 us
    psum x1, waiting for transfers between devices, broadcast(): return lax.psum(jnp.where(mine, shard, jnp.zeros_like(shard)), axis)  82.8 us
    all_to_all x1, waiting for transfers between devices, per_device(): lax.all_to_all(to_buckets(tail_rows, position, layout), 'rel', split_axis...  70.6 us
    scatter x2, other arithmetic, to_buckets(): filled = jnp.zeros(flat_shape, values.dtype).at[position].set(values)  50.3 us
    gather x2, local copies, waits for them, and re-layouts, from_buckets(): return stacked.reshape((-1,) + stacked.shape[3:])[position]  34.1 us
    psum x1, waiting for transfers between devices, per_device(): lax.psum(partial_value.astype(jnp.bfloat16), 'grp').astype(jnp.float32)  29.9 us
    all_to_all x1, waiting for transfers between devices, per_device(): lax.all_to_all(head_back, 'rel', split_axis=0, concat_axis=0, tiled=True)  23.6 us
    dot_general x1, matrix products, score_rows(): jnp.dot(query_rows, negatives.T, preferred_element_type=jnp.float32)  16.5 us
  transfers between devices with their start and end apart: 6, of which 5 were waited for; matrix products, arithmetic and copies ran while one was open for 19% of the time, Pallas kernels for 0%

commit v1 on v0

--- a/solution.py
+++ b/solution.py
@@ -4,6 +4,22 @@
 from jax.sharding import PartitionSpec as P
 
 LEARNING_RATE = 1.0
+
+
+def exchange_in_pairs(shard, axis, split, join):
+    ways, here = (lax.axis_size(axis), lax.axis_index(axis))
+    width = shard.shape[split] // ways
+    shape = list(shard.shape)
+    shape[split] = width
+    height = shape[join]
+    shape[join] = height * ways
+    full = jnp.zeros(shape, shard.dtype)
+    for mask in range(ways):
+        part = lax.dynamic_slice_in_dim(shard, (here ^ mask) * width, width, axis=split)
+        if mask:
+            part = lax.ppermute(part, axis, [(d, d ^ mask) for d in range(ways)])
+        full = lax.dynamic_update_slice_in_dim(full, part, (here ^ mask) * height, axis=join)
+    return full
 
 
 def broadcast(shard, axis, root):
@@ -78,7 +94,7 @@
     ).astype(jnp.bfloat16)
     partial_value, head_back = (partial_value, head_back)
     back_grads, back_losses = (
-        lax.all_to_all(head_back, "rel", split_axis=0, concat_axis=0, tiled=True),
+        exchange_in_pairs(head_back, "rel", 0, 0),
         lax.all_to_all(slot_losses.reshape(layout), "rel", split_axis=0, concat_axis=0, tiled=True),
     )
     head_grad = from_buckets(back_grads, position)

time: 506 us -> 549 us (1.085)
  the two profiles are of different devices: /device:TPU:0 before, /device:TPU:8 now
where the time goes in v1:
time: 549 us; the launch traced here: 541 us
  waiting for transfers between devices  320 us (58%)
  other arithmetic  76 us (14%)
  local copies, waits for them, and re-layouts  57.5 us (10%)
  matrix products  44.9 us (8%)
  starting transfers between devices  27.5 us (5%)
  between operations  15.1 us (3%)
    psum x1, waiting for transfers between devices, broadcast(): return lax.psum(jnp.where(mine, shard, jnp.zeros_like(shard)), axis)  93.3 us
    all_to_all x1, waiting for transfers between devices, per_device(): lax.all_to_all(to_buckets(tail_rows, position, layout), 'rel', split_axis...  92.5 us
    all_to_all x1, waiting for transfers between devices, per_device(): lax.all_to_all(to_buckets(head_rows, position, layout), 'rel', split_axis...  67.9 us
    scatter x2, other arithmetic, to_buckets(): filled = jnp.zeros(flat_shape, values.dtype).at[position].set(values)  50.3 us
    gather x2, local copies, waits for them, and re-layouts, from_buckets(): return stacked.reshape((-1,) + stacked.shape[3:])[position]  34.1 us
    all_to_all x1, waiting for transfers between devices, per_device(): lax.all_to_all(slot_losses.reshape(layout), 'rel', split_axis=0, concat_a...  33.9 us
    ppermute x7, waiting for transfers between devices, exchange_in_pairs(): part = lax.ppermute(part, axis, [(d, d ^ mask) for d in range(ways)])  32.8 us
    dot_general x1, matrix products, score_rows(): jnp.dot(query_rows, negatives.T, preferred_element_type=jnp.float32)  16.2 us
  transfers between devices with their start and end apart: 12, of which 6 were waited for; matrix products, arithmetic and copies ran while one was open for 16% of the time, Pallas kernels for 0%

profile of v1, /device:TPU:8, one launch (start us, length us, event | category | flops | bytes accessed | tf_op | source)
XLA Modules:
  0.0 541.4 jit_solution(917453968259011978)
XLA Ops:
  9.3 9.1 %reduce-window.6 = s32[32,16,128]{2,1,0:T(8,128)S(1)} reduce-window(s32[32,16,128]{2,1,0:T(8,128)S(1)} %fusion.31, s32[]{:T(128)} %constant.29.clone.1), window={size=1x1x128 pad=0_0x0_0x127_0}, to_apply=%region_0.0 | reduce-window | flops 8323072 | bytes 524292 | tf_op jit(solution)/shard_map/reduce-window
  20.6 27.6 %scatter_custom_fusion = bf16[4096,512]{1,0:T(8,128)(2,1)} fusion(s32[2048]{0:T(1024)S(1)} %bitcast.81, bf16[]{:T(256)} %constant.27.clone.1, pred[2048]{0:T(1024)(128)(4,1)S(1)} %compare_and_fusion.1, bf16[]{:T(256)} %constant.15.clone.2, bf16[1024,512]{1,0:T(8,128)(2,1)} %param.13, s32[2048]{0:T(1024)S(1)} %fusion.34), kind=kCustom, calls=%fused_computation.30 | custom fusion | flops 1048576 | bytes 5253124 | tf_op jit(solution)/shard_map/scatter | solution.py:53
  48.2 6.9 %all-to-all-start = ((bf16[8,4,128,512]{3,2,1,0:T(8,128)(2,1)}), bf16[8,4,128,512]{3,2,1,0:T(8,128)(2,1)}, u32[]{:S(2)}, u32[]{:S(2)}) async-start(bf16[8,4,128,512]{3,2,1,0:T(8,128)(2,1)} %bitcast.72), calls=%async_computation | async-start | bytes 8388608 | tf_op jit(solution)/shard_map/all_to_all | solution.py:75
  55.2 22.7 %scatter_custom_fusion.1 = bf16[4096,512]{1,0:T(8,128)(2,1)} fusion(s32[2048]{0:T(1024)S(1)} %bitcast.82, bf16[]{:T(256)} %constant.27.clone.1, pred[2048]{0:T(1024)(128)(4,1)S(1)} %compare_and_fusion, bf16[]{:T(256)} %constant.15.clone.2, bf16[1024,512]{1,0:T(8,128)(2,1)S(1)} %copy-done, s32[2048]{0:T(1024)S(1)} %fusion.35), kind=kCustom, calls=%fused_computation.28 | custom fusion | flops 1048576 | bytes 5253124 | tf_op jit(solution)/shard_map/scatter | solution.py:53
  77.9 67.9 %all-to-all-done = bf16[8,4,128,512]{3,2,1,0:T(8,128)(2,1)} async-done(((bf16[8,4,128,512]{3,2,1,0:T(8,128)(2,1)}), bf16[8,4,128,512]{3,2,1,0:T(8,128)(2,1)}, u32[]{:S(2)}, u32[]{:S(2)}) %all-to-all-start) | async-done | bytes 4194336 | tf_op jit(solution)/shard_map/all_to_all | solution.py:75
  145.8 7.0 %all-to-all-start.1 = ((bf16[8,4,128,512]{3,2,1,0:T(8,128)(2,1)}), bf16[8,4,128,512]{3,2,1,0:T(8,128)(2,1)}, u32[]{:S(2)}, u32[]{:S(2)}) async-start(bf16[8,4,128,512]{3,2,1,0:T(8,128)(2,1)} %bitcast.71), calls=%async_computation.1 | async-start | bytes 8388608 | tf_op jit(solution)/shard_map/all_to_all | solution.py:78
  154.6 92.5 %all-to-all-done.1 = bf16[8,4,128,512]{3,2,1,0:T(8,128)(2,1)} async-done(((bf16[8,4,128,512]{3,2,1,0:T(8,128)(2,1)}), bf16[8,4,128,512]{3,2,1,0:T(8,128)(2,1)}, u32[]{:S(2)}, u32[]{:S(2)}) %all-to-all-start.1) | async-done | bytes 4194336 | tf_op jit(solution)/shard_map/all_to_all | solution.py:78
  247.1 7.1 %multiply_reduce_fusion = (f32[8,4,128]{2,0,1:T(8,128)S(1)}, bf16[8,4,128,512]{3,2,0,1:T(8,128)(2,1)S(1)}) fusion(bf16[8,4,128,512]{3,2,1,0:T(8,128)(2,1)} %all-to-all-done.1, f32[4,512,512]{2,1,0:T(8,128)} %param.14, bf16[8,4,128,512]{3,2,1,0:T(8,128)(2,1)} %all-to-all-done), kind=kOutput, calls=%fused_computation.12 | convolution fusion | flops 2159013888 | bytes 16793600 | tf_op jit(solution)/shard_map/srcd,rde->srce/dot_general | solution.py:82
  254.2 2.5 copy.47
  256.7 93.3 %all-reduce.3.cloned.1.call-done = bf16[1024,512]{1,0:T(8,128)(2,1)} async-done(((bf16[1024,512]{1,0:T(8,128)(2,1)}), bf16[1024,512]{1,0:T(8,128)(2,1)}) %all-reduce.3.cloned.1.call-update) | async-done | bytes 1048592 | tf_op jit(solution)/shard_map/psum | solution.py:27
  350.0 16.2 %fusion = (f32[4096]{0:T(1024)S(1)}, f32[4096,1024]{0,1:T(8,128)}) fusion(bf16[4096,512]{1,0:T(8,128)(2,1)} %bitcast.73, bf16[1024,512]{1,0:T(8,128)(2,1)} %all-reduce.3.cloned.1.call-done), kind=kOutput, calls=%fused_computation.7 | convolution fusion | flops 4324323328 | bytes 22036480 | tf_op jit(solution)/shard_map/dot_general | solution.py:38
  366.3 3.4 copy_convert_fusion
  371.3 11.1 %fusion.2 = bf16[4096,512]{1,0:T(8,128)(2,1)} fusion(f32[8,4,128,512]{3,2,1,0:T(8,128)S(1)} %copy.51, bf16[1024,512]{1,0:T(8,128)(2,1)S(1)} %copy-done.5, f32[4096,1024]{0,1:T(8,128)} %get-tuple-element.19, f32[4096]{0:T(1024)S(1)} %bitcast.84), kind=kOutput, calls=%fused_computation.11 | convolution fusion | flops 4322230272 | bytes 30425088 | tf_op jit(solution)/shard_map/dot_general | solution.py:42
  382.4 4.6 fusion.12
  387.1 1.9 copy-done.1
  392.0 5.9 %bitcast_convert_fusion = bf16[4,512,512]{2,1,0:T(8,128)(2,1)} fusion(bf16[8,4,128,512]{3,2,1,0:T(8,128)(2,1)} %all-to-all-done, bf16[8,4,128,512]{3,2,1,0:T(8,128)(2,1)S(1)} %bitcast.86), kind=kOutput, calls=%fused_computation.18 | convolution fusion | flops 2148532224 | bytes 10485760 | tf_op jit(solution)/shard_map/srcd,srce->rde/dot_general | solution.py:89
  400.9 2.4 collective-permute-start.4
  403.9 4.1 all-to-all-start.2
  408.0 2.5 broadcast_in_dim.14
  410.5 1.9 bitcast_dynamic-update-slice_fusion
  412.4 33.9 %all-to-all-done.2 = bf16[8,4,128]{2,1,0:T(4,128)(2,1)S(1)} async-done(((bf16[8,4,128]{2,1,0:T(4,128)(2,1)}), bf16[8,4,128]{2,1,0:T(4,128)(2,1)S(1)}, u32[]{:S(2)}, u32[]{:S(2)}) %all-to-all-start.2) | async-done | bytes 8224 | tf_op jit(solution)/shard_map/all_to_all | solution.py:98
  446.3 22.1 %gather_fusion = bf16[2048]{0:T(1024)(128)(2,1)} fusion(bf16[4096]{0:T(1024)(128)(2,1)S(1)} %bitcast.70, s32[2048]{0:T(1024)S(1)} %broadcast_clamp_fusion), kind=kCustom, calls=%fused_computation.2 | custom fusion | bytes 16384 | tf_op jit(solution)/shard_map/gather | solution.py:58
  468.9 1.9 constant_dynamic-update-slice_fusion.5
  472.2 1.9 constant_dynamic-update-slice_fusion.4
  474.1 1.9 constant_dynamic-update-slice_fusion.3
  476.0 1.9 constant_dynamic-update-slice_fusion.2
  477.9 1.9 constant_dynamic-update-slice_fusion.1
  479.7 24.2 %collective-permute-done.5 = bf16[1,4,128,512]{3,2,1,0:T(8,128)(2,1)S(1)} collective-permute-done((bf16[1,4,128,512]{3,2,1,0:T(8,128)(2,1)S(1)}, bf16[1,4,128,512]{3,2,1,0:T(8,128)(2,1)S(1)}, u32[]{:S(2)}, u32[]{:S(2)}) %collective-permute-start.5) | collective-permute-done | bytes 524320 | tf_op jit(solution)/shard_map/ppermute | solution.py:20
  504.8 8.5 %collective-permute-done.6 = bf16[1,4,128,512]{3,2,1,0:T(8,128)(2,1)S(1)} collective-permute-done((bf16[1,4,128,512]{3,2,1,0:T(8,128)(2,1)S(1)}, bf16[1,4,128,512]{3,2,1,0:T(8,128)(2,1)S(1)}, u32[]{:S(2)}, u32[]{:S(2)}) %collective-permute-start.6) | collective-permute-done | bytes 524320 | tf_op jit(solution)/shard_map/ppermute | solution.py:20
  514.1 12.0 %gather_fusion.1 = bf16[2048,512]{1,0:T(8,128)(2,1)} fusion(bf16[4096,512]{1,0:T(8,128)(2,1)} %bitcast.28, s32[2048]{0:T(1024)S(1)} %broadcast_clamp_fusion), kind=kCustom, calls=%fused_computation.3 | custom fusion | bytes 4202496 | tf_op jit(solution)/shard_map/gather | solution.py:58
  526.1 2.1 fusion.4
  528.8 5.5 %fusion.5 = f32[4,512,512]{2,1,0:T(8,128)} fusion(f32[4,512,512]{2,1,0:T(8,128)} %param.14, bf16[4,512,512]{2,1,0:T(8,128)(2,1)} %all-reduce.5.cloned.1.call-done, f32[4,512]{1,0:T(4,128)S(1)} %get-tuple-element.5), kind=kLoop, calls=%fused_computation.17 | loop fusion | flops 3145728 | bytes 10493952 | tf_op jit(solution)/shard_map/sub | solution.py:48
  (51 shorter events, 18.0 us)
Async XLA Ops:
  48.2 6.9 %copy-start.3 = (s32[2048]{0:T(1024)S(1)}, s32[2048]{0:T(1024)}, u32[]{:S(2)}) copy-start(s32[2048]{0:T(1024)} %param.11) | copy-start | bytes 24580
  48.2 7.0 %copy-start = (bf16[1024,512]{1,0:T(8,128)(2,1)S(1)}, bf16[1024,512]{1,0:T(8,128)(2,1)}, u32[]{:S(2)}) copy-start(bf16[1024,512]{1,0:T(8,128)(2,1)} %param.13) | copy-start | bytes 3145732
  48.2 97.6 %all-to-all-start = ((bf16[8,4,128,512]{3,2,1,0:T(8,128)(2,1)}), bf16[8,4,128,512]{3,2,1,0:T(8,128)(2,1)}, u32[]{:S(2)}, u32[]{:S(2)}) async-start(bf16[8,4,128,512]{3,2,1,0:T(8,128)(2,1)} %bitcast.72), calls=%async_computation | async-start | bytes 8388608 | tf_op jit(solution)/shard_map/all_to_all | solution.py:75
  145.8 101.3 %all-to-all-start.1 = ((bf16[8,4,128,512]{3,2,1,0:T(8,128)(2,1)}), bf16[8,4,128,512]{3,2,1,0:T(8,128)(2,1)}, u32[]{:S(2)}, u32[]{:S(2)}) async-start(bf16[8,4,128,512]{3,2,1,0:T(8,128)(2,1)} %bitcast.71), calls=%async_computation.1 | async-start | bytes 8388608 | tf_op jit(solution)/shard_map/all_to_all | solution.py:78
  152.8 197.2 %all-reduce.3.cloned.1.call-start = ((), (), s32[]{:S(2)}) async-start(), calls=%async_computation.3 | async-start | bytes 2097152 | tf_op jit(solution)/shard_map/psum | solution.py:27
  154.5 371.6 %all-reduce.5.cloned.1.call-start = ((), (), s32[]{:S(2)}) async-start(), calls=%async_computation.4 | async-start | bytes 4194304 | tf_op jit(solution)/shard_map/psum | solution.py:102
  369.7 1.6 copy-start.5
  371.3 11.1 %copy-start.2 = (f32[4,512,512]{2,1,0:T(8,128)S(1)}, f32[4,512,512]{2,1,0:T(8,128)}, u32[]{:S(2)}) copy-start(f32[4,512,512]{2,1,0:T(8,128)} %param.14) | copy-start | bytes 12582916
  387.0 1.9 copy-start.1
  389.0 3.0 copy-start.6
  390.0 78.3 %collective-permute-start = (bf16[1,4,128,512]{3,2,1,0:T(8,128)(2,1)}, bf16[1,4,128,512]{3,2,1,0:T(8,128)(2,1)}, u32[]{:S(2)}, u32[]{:S(2)}) collective-permute-start(bf16[1,4,128,512]{3,2,1,0:T(8,128)(2,1)} %get-tuple-element.13), channel_id=1, source_target_pairs={{0,1},{1,0},{2,3},{3,2},{4,5},{5,4},{6,7},{7,6},{8,9},{9,8},{10,11... | collective-permute-start | bytes 1572872 | tf_op jit(solution)/shard_map/ppermute | solution.py:20
  391.4 79.3 %collective-permute-start.1 = (bf16[1,4,128,512]{3,2,1,0:T(8,128)(2,1)S(1)}, bf16[1,4,128,512]{3,2,1,0:T(8,128)(2,1)}, u32[]{:S(2)}, u32[]{:S(2)}) collective-permute-start(bf16[1,4,128,512]{3,2,1,0:T(8,128)(2,1)S(1)} %get-tuple-element.12), channel_id=1, source_target_pairs={{0,2},{1,3},{2,0},{3,1},{4,6},{5,7},{6,4},{7,5},{8,10},{9,11},{10,... | collective-permute-start | bytes 1572872 | tf_op jit(solution)/shard_map/ppermute | solution.py:20
  397.9 76.2 %collective-permute-start.2 = (bf16[1,4,128,512]{3,2,1,0:T(8,128)(2,1)S(1)}, bf16[1,4,128,512]{3,2,1,0:T(8,128)(2,1)}, u32[]{:S(2)}, u32[]{:S(2)}) collective-permute-start(bf16[1,4,128,512]{3,2,1,0:T(8,128)(2,1)S(1)} %get-tuple-element.11), channel_id=1, source_target_pairs={{0,3},{1,2},{2,1},{3,0},{4,7},{5,6},{6,5},{7,4},{8,11},{9,10},{10,... | collective-permute-start | bytes 1572872 | tf_op jit(solution)/shard_map/ppermute | solution.py:20
  399.5 76.5 %collective-permute-start.3 = (bf16[1,4,128,512]{3,2,1,0:T(8,128)(2,1)S(1)}, bf16[1,4,128,512]{3,2,1,0:T(8,128)(2,1)}, u32[]{:S(2)}, u32[]{:S(2)}) collective-permute-start(bf16[1,4,128,512]{3,2,1,0:T(8,128)(2,1)S(1)} %get-tuple-element.10), channel_id=1, source_target_pairs={{0,4},{1,5},{2,6},{3,7},{4,0},{5,1},{6,2},{7,3},{8,12},{9,13},{10,... | collective-permute-start | bytes 1572872 | tf_op jit(solution)/shard_map/ppermute | solution.py:20
  400.9 77.0 %collective-permute-start.4 = (bf16[1,4,128,512]{3,2,1,0:T(8,128)(2,1)S(1)}, bf16[1,4,128,512]{3,2,1,0:T(8,128)(2,1)}, u32[]{:S(2)}, u32[]{:S(2)}) collective-permute-start(bf16[1,4,128,512]{3,2,1,0:T(8,128)(2,1)S(1)} %get-tuple-element.9), channel_id=1, source_target_pairs={{0,5},{1,4},{2,7},{3,6},{4,1},{5,0},{6,3},{7,2},{8,13},{9,12},{10,... | collective-permute-start | bytes 1572872 | tf_op jit(solution)/shard_map/ppermute | solution.py:20
  403.9 42.4 %all-to-all-start.2 = ((bf16[8,4,128]{2,1,0:T(4,128)(2,1)}), bf16[8,4,128]{2,1,0:T(4,128)(2,1)S(1)}, u32[]{:S(2)}, u32[]{:S(2)}) async-start(bf16[8,4,128]{2,1,0:T(4,128)(2,1)} %copy.49), calls=%async_computation.2 | async-start | bytes 16384 | tf_op jit(solution)/shard_map/all_to_all | solution.py:98
  468.4 35.6 %collective-permute-start.5 = (bf16[1,4,128,512]{3,2,1,0:T(8,128)(2,1)S(1)}, bf16[1,4,128,512]{3,2,1,0:T(8,128)(2,1)S(1)}, u32[]{:S(2)}, u32[]{:S(2)}) collective-permute-start(bf16[1,4,128,512]{3,2,1,0:T(8,128)(2,1)S(1)} %get-tuple-element.8), channel_id=1, source_target_pairs={{0,6},{1,7},{2,4},{3,5},{4,2},{5,3},{6,0},{7,1},{8,14},{9,15},{10,... | collective-permute-start | bytes 1572872 | tf_op jit(solution)/shard_map/ppermute | solution.py:20
  470.7 42.5 %collective-permute-start.6 = (bf16[1,4,128,512]{3,2,1,0:T(8,128)(2,1)S(1)}, bf16[1,4,128,512]{3,2,1,0:T(8,128)(2,1)S(1)}, u32[]{:S(2)}, u32[]{:S(2)}) collective-permute-start(bf16[1,4,128,512]{3,2,1,0:T(8,128)(2,1)S(1)} %get-tuple-element.7), channel_id=1, source_target_pairs={{0,7},{1,6},{2,5},{3,4},{4,3},{5,2},{6,1},{7,0},{8,15},{9,14},{10,... | collective-permute-start | bytes 1572872 | tf_op jit(solution)/shard_map/ppermute | solution.py:20
  514.1 14.1 %copy-start.4 = (f32[4,512]{1,0:T(4,128)S(1)}, f32[4,512]{1,0:T(4,128)}, u32[]{:S(2)}) copy-start(f32[4,512]{1,0:T(4,128)} %param.15) | copy-start | bytes 24580
Sparse Core Ops, SparseCore 0:
  159.4 190.6 all-reduce.2
  398.1 50.3 all-reduce.4
